TPU v7x, 256 devices: a whole 4x4x8 slice. The times are simulated.
256 devices in a mesh: dp: 16 (over y, x_hi, core), tensor: 16 (over x_lo, z).
Axes of the slice: x: 4 (x_hi: 2, x_lo: 2; x = x_hi * 2 + x_lo), y: 4, z: 8, core: 2. Of those that a mesh axis runs over, the one named last changes fastest.
Arguments:
- tokens: bfloat16 [768, 6144], P('dp', 'tensor'), may hold values from -6 to 6
- routes: int32 [768, 2], P('dp'), may hold values from 0 to 3, all different within a row; in each aligned block of 48 rows (0 to 47, 48 to 95, ...) at most 32 rows name the same one
- gate_weights: bfloat16 [768, 2], P('dp'), may hold values from 0.25 to 1
- gate_matrix: bfloat16 [16, 6144, 2048], P('dp', None, 'tensor'), may hold values from -0.078125 to 0.078125
- up_matrix: bfloat16 [16, 6144, 2048], P('dp', None, 'tensor'), may hold values from -0.078125 to 0.078125
- down_matrix: bfloat16 [16, 2048, 6144], P('dp', 'tensor'), may hold values from -0.0625 to 0.0625
- cotangent: bfloat16 [768, 6144], P('dp', 'tensor'), may hold values from -6 to 6
Outputs:
- layer_out: bfloat16 [768, 6144], P('dp', 'tensor')
- token_gradient: bfloat16 [768, 6144], P('dp', 'tensor')
- gate_gradient: bfloat16 [16, 6144, 2048], P('dp', None, 'tensor')
- up_gradient: bfloat16 [16, 6144, 2048], P('dp', None, 'tensor')
- down_gradient: bfloat16 [16, 2048, 6144], P('dp', 'tensor')
Inputs may be any that keep to these rules, and one draw needn't show every extreme that they name: `routes`: within the rows of one dp index (aligned blocks of 48 rows) no expert is named by more than 32 rows, and in some such block one expert is named by exactly 32; the two experts of a row differ.
All inputs are finite; a program needn't handle non-finite values.
Results may differ from a plain program's by a relative error of at most 0.018.
Values may be sent and summed in bfloat16 or wider, within the bound.
No kernel may reach another device: no remote copies, remote signals or barrier semaphores. Data moves between devices by JAX's collectives and lax.ppermute only.
A program may use at most 128 MiB of HBM per device.

v0:
```python
import jax
import jax.numpy as jnp
from jax import lax
from jax.experimental.layout import Layout, with_layout_constraint
from jax.sharding import Mesh, NamedSharding, PartitionSpec as P

EXPERTS = 4
CAP = 32
DP = ("y", "xhi", "core")
TN = ("xlo", "z")
SRC = ("y", "xhi")
precise = lax.Precision.HIGHEST


def slot_tables(routes, gate_weights, capacity):
    experts = jnp.arange(EXPERTS, dtype=jnp.int32)
    hit_mask = routes[:, :, None] == experts[None, None, :]
    chosen = jnp.any(hit_mask, axis=1)
    weights = jnp.sum(
        jnp.where(hit_mask, gate_weights.astype(jnp.float32)[:, :, None], jnp.float32(0.0)), axis=1
    )
    places = jnp.cumsum(chosen.astype(jnp.int32), axis=0) - 1
    columns = jnp.arange(capacity, dtype=jnp.int32)
    onehot = (places[:, :, None] == columns[None, None, :]) & chosen[:, :, None]
    return (onehot, weights)


def per_device(tokens, routes, gate_weights, gate_matrix, up_matrix, down_matrix, cotangent):
    feature_cols = tokens.shape[1]
    n_src = lax.axis_size(SRC)
    expert_span = n_src // EXPERTS
    onehot, weights = slot_tables(routes, gate_weights, CAP)
    member = onehot.astype(jnp.float32)
    scaled = member * weights[:, :, None]

    def spread(slot_table):
        widened = jnp.broadcast_to(
            slot_table[:, :, None, :], (slot_table.shape[0], EXPERTS, expert_span, CAP)
        )
        return widened.reshape(slot_table.shape[0], EXPERTS * expert_span * CAP)

    member_wide = spread(member)
    scaled_wide = spread(scaled)
    token_send = jnp.einsum(
        "tr,tc->rc", member_wide.astype(jnp.bfloat16), tokens, preferred_element_type=jnp.float32
    ).astype(jnp.bfloat16)
    grad_send = jnp.einsum(
        "tr,tc->rc", scaled_wide, cotangent.astype(jnp.float32), precision=precise
    ).astype(jnp.bfloat16)
    send = jnp.concatenate(
        [token_send.reshape(n_src, CAP, feature_cols), grad_send.reshape(n_src, CAP, feature_cols)],
        axis=1,
    )
    recv = lax.all_to_all(send, SRC, split_axis=0, concat_axis=0, tiled=True)
    mine = recv.reshape(n_src, 2, CAP, feature_cols).transpose(1, 0, 2, 3)
    mine = mine.reshape(2, n_src * CAP, feature_cols)
    mine_full = lax.all_gather(mine, TN, axis=2, tiled=True)
    pair = [(0, 1), (1, 0)]
    gate_local = gate_matrix[0]
    up_local = up_matrix[0]
    down_local = down_matrix[0]
    gu_local = jnp.concatenate([gate_local, up_local], axis=1)
    gu_other, down_other = lax.ppermute((gu_local, down_local), "core", pair)

    def forward(pre, gu_w, down_w):
        width = pre.shape[1] // 2
        gate_pre, up_pre = (pre[:, :width], pre[:, width:])
        sigmoid_gate = jax.nn.sigmoid(gate_pre)
        activated = gate_pre * sigmoid_gate
        hidden = (activated * up_pre).astype(jnp.bfloat16)
        out_t = jnp.einsum("hd,rh->dr", down_w, hidden, preferred_element_type=jnp.float32).astype(
            jnp.bfloat16
        )
        out_t = with_layout_constraint(out_t, Layout(major_to_minor=(0, 1)))
        return (gate_pre, up_pre, sigmoid_gate, activated, hidden, out_t)

    def backward(hidden_grad, gate_pre, up_pre, sigmoid_gate, activated, gu_w, down_w):
        gate_grad = (
            hidden_grad * up_pre * sigmoid_gate * (1.0 + gate_pre * (1.0 - sigmoid_gate))
        ).astype(jnp.bfloat16)
        up_grad = (hidden_grad * activated).astype(jnp.bfloat16)
        both_grad = jnp.concatenate([gate_grad, up_grad], axis=1)
        back_t = jnp.einsum(
            "dh,rh->dr", gu_w, both_grad, preferred_element_type=jnp.float32
        ).astype(jnp.bfloat16)
        back_t = with_layout_constraint(back_t, Layout(major_to_minor=(0, 1)))
        return (gate_grad, up_grad, back_t)

    rows, grads = (mine_full[0], mine_full[1])
    own_w = (gu_local, down_local)
    other_w = (gu_other, down_other)
    width = gu_local.shape[1]
    pre_both = jnp.dot(
        rows, jnp.concatenate([gu_local, gu_other], axis=1), preferred_element_type=jnp.float32
    )
    hgrad_both = jnp.einsum(
        "rd,hd->rh",
        grads,
        jnp.concatenate([down_local, down_other], axis=0),
        preferred_element_type=jnp.float32,
    )
    f_own = forward(pre_both[:, :width], *own_w)
    f_other = forward(pre_both[:, width:], *other_w)
    b_own = backward(hgrad_both[:, : width // 2], *f_own[:4], *own_w)
    b_other = backward(hgrad_both[:, width // 2 :], *f_other[:4], *other_w)
    own = jnp.concatenate([f_own[5], b_own[2]], axis=1)
    other = jnp.concatenate([f_other[5], b_other[2]], axis=1)
    summed = (own.astype(jnp.float32) + other.astype(jnp.float32)).astype(jnp.bfloat16)
    scattered = lax.psum_scatter(summed, TN, scatter_dimension=0, tiled=True)
    n_rows = f_own[5].shape[1]
    out_rows = scattered[:, :n_rows].T
    back_rows = scattered[:, n_rows:].T

    def weight_grads(f, b):
        return (
            jnp.einsum("rd,rh->dh", rows, b[0], preferred_element_type=jnp.float32),
            jnp.einsum("rd,rh->dh", rows, b[1], preferred_element_type=jnp.float32),
            jnp.einsum("rh,rd->hd", f[4], grads, preferred_element_type=jnp.float32),
        )

    w_own = weight_grads(f_own, b_own)
    w_recv = lax.ppermute(weight_grads(f_other, b_other), "core", pair)
    gate_gradient = (w_own[0] + w_recv[0]).astype(jnp.bfloat16)[None]
    up_gradient = (w_own[1] + w_recv[1]).astype(jnp.bfloat16)[None]
    down_gradient = (w_own[2] + w_recv[2]).astype(jnp.bfloat16)[None]
    done = jnp.concatenate(
        [out_rows.reshape(n_src, CAP, feature_cols), back_rows.reshape(n_src, CAP, feature_cols)],
        axis=1,
    )
    returned = lax.all_to_all(done, SRC, split_axis=0, concat_axis=0, tiled=True).astype(
        jnp.float32
    )
    returned_out = returned[:, :CAP].reshape(-1, feature_cols)
    returned_back = returned[:, CAP:].reshape(-1, feature_cols)
    layer_out = jnp.dot(
        scaled_wide, returned_out, precision=precise, preferred_element_type=jnp.float32
    ).astype(jnp.bfloat16)
    token_gradient = jnp.dot(
        member_wide, returned_back, precision=precise, preferred_element_type=jnp.float32
    ).astype(jnp.bfloat16)
    return (layer_out, token_gradient, gate_gradient, up_gradient, down_gradient)


def solution(mesh):
    sizes = dict(mesh.shape)
    sub = Mesh(mesh.devices.reshape(sizes["dp"] // 4, 2, 2, 2, sizes["tensor"] // 2), DP + TN)
    in_specs = (
        P(DP, TN),
        P(DP, None),
        P(DP, None),
        P(DP, None, TN),
        P(DP, None, TN),
        P(DP, TN, None),
        P(DP, TN),
    )
    out_specs = (P(DP, TN), P(DP, TN), P(DP, None, TN), P(DP, None, TN), P(DP, TN, None))
    placed = (
        P("dp", "tensor"),
        P("dp", "tensor"),
        P("dp", None, "tensor"),
        P("dp", None, "tensor"),
        P("dp", "tensor", None),
    )
    inner = jax.shard_map(
        per_device, mesh=sub, in_specs=in_specs, out_specs=out_specs, check_vma=False
    )

    def run(*args):
        outs = inner(*args)
        return tuple(
            (lax.with_sharding_constraint(o, NamedSharding(mesh, p)) for o, p in zip(outs, placed))
        )

    return run
```

profile of v0, /device:TPU:8, one launch (start us, length us, event | category | flops | bytes accessed | tf_op | source)
XLA Modules:
  0.0 240.8 jit_solution(1196696518437505472)
XLA Ops:
  7.2 0.0 copy-start
  7.2 0.0 copy-start.5
  7.2 0.0 copy-start.3
  7.2 0.0 all-gather.2.cloned.1.call-start
  7.3 0.8 fusion.32
  8.1 0.1 copy.33
  8.2 0.1 reduce_window_sum.11
  8.3 0.1 copy.34
  8.4 0.7 convert_element_type.89
  9.0 0.7 select_reduce_fusion
  9.7 0.0 copy-start.9
  9.8 0.3 convolution_convert_fusion.5
  10.1 0.9 convolution_convert_fusion.4
  11.1 15.8 %all_to_all.10 = bf16[8,64,384]{2,1,0:T(8,128)(2,1)S(1)} all-to-all(bf16[8,64,384]{2,1,0:T(8,128)(2,1)S(1)} %pad_maximum_fusion.1), channel_id=1, replica_groups=mesh['y'=4,'xhi'=2,'core'=2,'xlo'=2,'z'=8] {'y','xhi'}, dimensions={0} | all-to-all | bytes 786432 | tf_op jit(solution)/shard_map/all_to_all | solution.py:54
  27.0 0.8 copy.35
  27.8 0.0 all-gather.2.cloned.1.call-update
  27.8 0.0 reduce-scatter.2.cloned.1.call-start
  27.8 0.3 pad_maximum_fusion
  28.2 0.1 collective-permute-start
  28.3 0.5 collective-permute-start.1
  28.8 5.1 %collective-permute-done = bf16[6144,256]{1,0:T(8,128)(2,1)S(1)} collective-permute-done((bf16[6144,256]{1,0:T(8,128)(2,1)S(1)}, bf16[6144,256]{1,0:T(8,128)(2,1)S(1)}, u32[]{:S(2)}, u32[]{:S(2)}) %collective-permute-start) | collective-permute-done | bytes 3145760 | tf_op jit(solution)/shard_map/ppermute | solution.py:63
  33.9 76.6 %all-gather.2.cloned.1.call-done = bf16[2,256,6144]{2,1,0:T(8,128)(2,1)} async-done(((bf16[2,256,384]{2,1,0:T(8,128)(2,1)}), bf16[2,256,6144]{2,1,0:T(8,128)(2,1)}) %all-gather.2.cloned.1.call-update) | async-done | bytes 6291472 | tf_op jit(solution)/shard_map/all_gather | solution.py:57
  110.6 4.8 %fusion.8 = f32[256,512]{1,0:T(8,128)S(1)} fusion(bf16[6144,256]{1,0:T(8,128)(2,1)S(1)} %collective-permute-done, bf16[6144,128]{1,0:T(8,128)(2,1)} %bitcast.66, bf16[6144,128]{1,0:T(8,128)(2,1)} %bitcast.69, bf16[2,256,6144]{2,1,0:T(8,128)(2,1)} %all-gather.2.cloned.1.call-done), kind=kOutput, calls=%fused_computation.16 | convolution fusion | flops 1629487104 | bytes 9961472 | tf_op jit(solution)/shard_map/dot_general | solution.py:93
  115.4 0.0 collective-permute-done.1
  115.4 2.9 %fusion.14 = f32[256,256]{1,0:T(8,128)S(1)} fusion(bf16[128,6144]{1,0:T(8,128)(2,1)} %collective-permute-done.1, bf16[128,6144]{1,0:T(8,128)(2,1)} %bitcast.10, bf16[2,256,6144]{2,1,0:T(8,128)(2,1)S(1)} %copy-done.2), kind=kOutput, calls=%fused_computation.25 | convolution fusion | flops 811597824 | bytes 6553600 | tf_op jit(solution)/shard_map/rd,hd->rh/dot_general | solution.py:96
  118.3 0.0 copy-start.4
  118.3 0.0 copy-start.6
  118.3 0.2 multiply_convert_fusion.1
  118.5 0.0 copy-start.11
  118.5 0.0 copy-start.13
  118.6 0.0 copy-start.7
  118.6 2.6 %fusion = bf16[6144,256]{1,0:T(8,128)(2,1)S(1)} fusion(bf16[256,128]{1,0:T(8,128)(2,1)S(1)} %get-tuple-element.10, bf16[1,128,6144]{2,1,0:T(8,128)(2,1)} %param.12), kind=kOutput, calls=%fused_computation.5 | convolution fusion | flops 404226048 | bytes 4784128 | tf_op jit(solution)/shard_map/hd,rh->dr/dot_general | solution.py:71
  121.2 1.0 convolution_convert_fusion.2
  122.2 0.0 copy-done.11
  122.2 0.0 copy-done.13
  122.3 2.4 %fusion.1 = bf16[6144,256]{1,0:T(8,128)(2,1)S(1)} fusion(bf16[256,128]{1,0:T(8,128)(2,1)S(1)} %get-tuple-element.9, bf16[128,6144]{1,0:T(8,128)(2,1)} %collective-permute-done.1), kind=kOutput, calls=%fused_computation.6 | convolution fusion | flops 404226048 | bytes 4784128 | tf_op jit(solution)/shard_map/hd,rh->dr/dot_general | solution.py:71
  124.7 1.0 convolution_convert_fusion
  125.7 3.9 %add_convert_fusion = bf16[6144,512]{1,0:T(8,128)(2,1)} fusion(bf16[6144,256]{1,0:T(8,128)(2,1)S(1)} %convolution_convert_fusion.2, bf16[6144,256]{1,0:T(8,128)(2,1)S(1)} %fusion, bf16[6144,256]{1,0:T(8,128)(2,1)S(1)} %convolution_convert_fusion, bf16[6144,256]{1,0:T(8,128)(2,1)S(1)} %fusion.1), kind=kLoop, calls=%fused_computation | loop fusion | flops 31457280 | bytes 18874368 | tf_op jit(solution)/shard_map/convert_element_type | solution.py:108
  129.6 0.0 reduce-scatter.2.cloned.1.call-update
  129.6 0.8 copy-done.8
  130.5 3.1 %fusion.19 = f32[6144,128]{1,0:T(8,128)S(1)} fusion(bf16[256,128]{1,0:T(8,128)(2,1)S(1)} %copy-done.8, bf16[2,256,6144]{2,1,0:T(8,128)(2,1)} %all-gather.2.cloned.1.call-done), kind=kOutput, calls=%fused_computation.30 | convolution fusion | flops 402653184 | bytes 6356992 | tf_op jit(solution)/shard_map/rd,rh->dh/dot_general | solution.py:117
  133.5 0.1 collective-permute-start.3
  133.7 0.1 slice-done.1
  133.8 1.0 fusion.20
  134.8 0.0 copy-start.14
  134.8 0.7 collective-permute-start.2
  135.5 2.2 fusion.18
  137.7 0.1 collective-permute-start.4
  137.8 1.5 collective-permute-done.3
  139.3 2.2 fusion.6
  141.5 2.2 collective-permute-done.2
  143.8 0.0 copy-done.12
  143.8 2.2 fusion.7
  146.0 68.6 %reduce-scatter.2.cloned.1.call-done = bf16[384,512]{1,0:T(8,128)(2,1)} async-done(((bf16[6144,512]{1,0:T(8,128)(2,1)}), bf16[384,512]{1,0:T(8,128)(2,1)}) %reduce-scatter.2.cloned.1.call-update) | async-done | bytes 393232 | tf_op jit(solution)/shard_map/reduce_scatter | solution.py:109
  214.7 1.0 slice_bitcast_fusion.11
  215.7 0.2 copy.38
  215.9 0.2 copy.39
  216.0 0.8 pad_maximum_fusion.2
  216.8 7.5 %all-to-all-start.1 = ((bf16[8,64,384]{2,1,0:T(8,128)(2,1)}), bf16[8,64,384]{2,1,0:T(8,128)(2,1)S(1)}, u32[]{:S(2)}, u32[]{:S(2)}) async-start(bf16[8,64,384]{2,1,0:T(8,128)(2,1)} %pad_maximum_fusion.2), calls=%async_computation.2 | async-start | bytes 786432 | tf_op jit(solution)/shard_map/all_to_all | solution.py:130
  224.4 0.0 collective-permute-done.4
  224.4 4.6 %fusion.5 = bf16[1,128,6144]{2,1,0:T(8,128)(2,1)} fusion(f32[128,6144]{1,0:T(8,128)} %collective-permute-done.4, bf16[256,128]{1,0:T(8,128)(2,1)S(1)} %get-tuple-element.10, bf16[2,256,6144]{2,1,0:T(8,128)(2,1)} %all-gather.2.cloned.1.call-done), kind=kOutput, calls=%fused_computation.13 | convolution fusion | flops 404226048 | bytes 7929856 | tf_op jit(solution)/shard_map/rh,rd->hd/dot_general | solution.py:118
  229.0 3.1 %all-to-all-done.1 = bf16[8,64,384]{2,1,0:T(8,128)(2,1)S(1)} async-done(((bf16[8,64,384]{2,1,0:T(8,128)(2,1)}), bf16[8,64,384]{2,1,0:T(8,128)(2,1)S(1)}, u32[]{:S(2)}, u32[]{:S(2)}) %all-to-all-start.1) | async-done | bytes 393248 | tf_op jit(solution)/shard_map/all_to_all | solution.py:130
  232.2 0.9 convolution_convert_fusion.7
  233.1 0.9 convolution_convert_fusion.6
  (29 shorter events, 0.2 us)
Async XLA Ops:
  7.2 2.6 %copy-start = (bf16[48,384]{1,0:T(8,128)(2,1)S(1)}, bf16[48,384]{1,0:T(8,128)(2,1)}, u32[]{:S(2)}) copy-start(bf16[48,384]{1,0:T(8,128)(2,1)} %param.13) | copy-start | bytes 110596
  7.2 20.6 %copy-start.5 = (bf16[1,6144,128]{2,1,0:T(8,128)(2,1)S(1)}, bf16[1,6144,128]{2,1,0:T(8,128)(2,1)}, u32[]{:S(2)}) copy-start(bf16[1,6144,128]{2,1,0:T(8,128)(2,1)} %param.10) | copy-start | bytes 4718596
  7.2 20.6 %copy-start.3 = (bf16[1,6144,128]{2,1,0:T(8,128)(2,1)S(1)}, bf16[1,6144,128]{2,1,0:T(8,128)(2,1)}, u32[]{:S(2)}) copy-start(bf16[1,6144,128]{2,1,0:T(8,128)(2,1)} %param.11) | copy-start | bytes 4718596
  7.2 103.4 %all-gather.2.cloned.1.call-start = ((), (), s32[]{:S(2)}) async-start(), calls=%async_computation.3 | async-start | bytes 6684672 | tf_op jit(solution)/shard_map/all_gather | solution.py:57
  9.7 1.3 copy-start.9
  27.8 186.9 %reduce-scatter.2.cloned.1.call-start = ((), (), s32[]{:S(2)}) async-start(), calls=%async_computation.4 | async-start | bytes 6684672 | tf_op jit(solution)/shard_map/reduce_scatter | solution.py:109
  28.2 5.7 %collective-permute-start = (bf16[6144,256]{1,0:T(8,128)(2,1)S(1)}, bf16[6144,256]{1,0:T(8,128)(2,1)S(1)}, u32[]{:S(2)}, u32[]{:S(2)}) collective-permute-start(bf16[6144,256]{1,0:T(8,128)(2,1)S(1)} %pad_maximum_fusion), channel_id=1, source_target_pairs={{0,16},{16,0},{1,17},{17,1},{2,18},{18,2},{3,19},{19,3},{4,20},{20... | collective-permute-start | bytes 9437192 | tf_op jit(solution)/shard_map/ppermute | solution.py:63
  28.3 87.1 %collective-permute-start.1 = (bf16[128,6144]{1,0:T(8,128)(2,1)}, bf16[128,6144]{1,0:T(8,128)(2,1)}, u32[]{:S(2)}, u32[]{:S(2)}) collective-permute-start(bf16[128,6144]{1,0:T(8,128)(2,1)} %bitcast.10), channel_id=1, source_target_pairs={{0,16},{16,0},{1,17},{17,1},{2,18},{18,2},{3,19},{19,3},{4,20},{20... | collective-permute-start | bytes 4718600 | tf_op jit(solution)/shard_map/ppermute | solution.py:63
  110.6 4.8 %copy-start.2 = (bf16[2,256,6144]{2,1,0:T(8,128)(2,1)S(1)}, bf16[2,256,6144]{2,1,0:T(8,128)(2,1)}, u32[]{:S(2)}) copy-start(bf16[2,256,6144]{2,1,0:T(8,128)(2,1)} %all-gather.2.cloned.1.call-done) | copy-start | bytes 18874372
  118.3 2.9 %copy-start.4 = (bf16[1,6144,128]{2,1,0:T(8,128)(2,1)S(1)}, bf16[1,6144,128]{2,1,0:T(8,128)(2,1)}, u32[]{:S(2)}) copy-start(bf16[1,6144,128]{2,1,0:T(8,128)(2,1)} %param.11) | copy-start | bytes 4718596
  118.3 2.9 %copy-start.6 = (bf16[1,6144,128]{2,1,0:T(8,128)(2,1)S(1)}, bf16[1,6144,128]{2,1,0:T(8,128)(2,1)}, u32[]{:S(2)}) copy-start(bf16[1,6144,128]{2,1,0:T(8,128)(2,1)} %param.10) | copy-start | bytes 4718596
  118.5 3.7 %copy-start.11 = (bf16[256,128]{1,0:T(8,128)(2,1)}, bf16[256,128]{1,0:T(8,128)(2,1)S(1)}, u32[]{:S(2)}) copy-start(bf16[256,128]{1,0:T(8,128)(2,1)S(1)} %get-tuple-element.8) | copy-start | bytes 196612
  118.5 3.7 %copy-start.13 = (bf16[256,128]{1,0:T(8,128)(2,1)}, bf16[256,128]{1,0:T(8,128)(2,1)S(1)}, u32[]{:S(2)}) copy-start(bf16[256,128]{1,0:T(8,128)(2,1)S(1)} %get-tuple-element.6) | copy-start | bytes 196612
  118.6 6.1 %copy-start.7 = (bf16[256,128]{1,0:T(8,128)(2,1)}, bf16[256,128]{1,0:T(8,128)(2,1)S(1)}, u32[]{:S(2)}) copy-start(bf16[256,128]{1,0:T(8,128)(2,1)S(1)} %get-tuple-element.7) | copy-start | bytes 196612
  129.6 0.8 copy-start.8
  129.6 4.0 %slice-start = ((s8[6291456]{0:T(1024)(128)(4,1)}), s8[2097152]{0:T(1024)(128)(4,1)S(1)}, s32[]{:S(2)}) async-start(s8[6291456]{0:T(1024)(128)(4,1)} %bitcast.62), calls=%async_computation.5 | async-start | bytes 4194304
  130.5 3.3 %slice-start.1 = ((s8[6291456]{0:T(1024)(128)(4,1)}), s8[4194304]{0:T(1024)(128)(4,1)S(1)}, s32[]{:S(2)}) async-start(s8[6291456]{0:T(1024)(128)(4,1)} %bitcast.62), calls=%async_computation.6 | async-start | bytes 8388608
  133.5 5.7 %collective-permute-start.3 = (f32[6144,128]{1,0:T(8,128)S(1)}, f32[6144,128]{1,0:T(8,128)S(1)}, u32[]{:S(2)}, u32[]{:S(2)}) collective-permute-start(f32[6144,128]{1,0:T(8,128)S(1)} %fusion.19), channel_id=1, source_target_pairs={{0,16},{16,0},{1,17},{17,1},{2,18},{18,2},{3,19},{19,3},{4,20},{20... | collective-permute-start | bytes 9437192 | tf_op jit(solution)/shard_map/ppermute | solution.py:122
  134.8 4.5 %copy-start.14 = (bf16[256,128]{1,0:T(8,128)(2,1)S(1)}, bf16[256,128]{1,0:T(8,128)(2,1)}, u32[]{:S(2)}) copy-start(bf16[256,128]{1,0:T(8,128)(2,1)} %copy-done.13) | copy-start | bytes 196612
  134.8 9.0 %collective-permute-start.2 = (f32[6144,128]{1,0:T(8,128)S(1)}, f32[6144,128]{1,0:T(8,128)S(1)}, u32[]{:S(2)}, u32[]{:S(2)}) collective-permute-start(f32[6144,128]{1,0:T(8,128)S(1)} %fusion.20), channel_id=1, source_target_pairs={{0,16},{16,0},{1,17},{17,1},{2,18},{18,2},{3,19},{19,3},{4,20},{20... | collective-permute-start | bytes 9437192 | tf_op jit(solution)/shard_map/ppermute | solution.py:122
  137.7 6.1 %copy-start.12 = (bf16[256,128]{1,0:T(8,128)(2,1)S(1)}, bf16[256,128]{1,0:T(8,128)(2,1)}, u32[]{:S(2)}) copy-start(bf16[256,128]{1,0:T(8,128)(2,1)} %copy-done.11) | copy-start | bytes 196612
  137.7 86.7 %collective-permute-start.4 = (f32[128,6144]{1,0:T(8,128)}, f32[128,6144]{1,0:T(8,128)}, u32[]{:S(2)}, u32[]{:S(2)}) collective-permute-start(f32[128,6144]{1,0:T(8,128)} %fusion.18), channel_id=1, source_target_pairs={{0,16},{16,0},{1,17},{17,1},{2,18},{18,2},{3,19},{19,3},{4,20},{20... | collective-permute-start | bytes 9437192 | tf_op jit(solution)/shard_map/ppermute | solution.py:122
  216.8 15.3 %all-to-all-start.1 = ((bf16[8,64,384]{2,1,0:T(8,128)(2,1)}), bf16[8,64,384]{2,1,0:T(8,128)(2,1)S(1)}, u32[]{:S(2)}, u32[]{:S(2)}) async-start(bf16[8,64,384]{2,1,0:T(8,128)(2,1)} %pad_maximum_fusion.2), calls=%async_computation.2 | async-start | bytes 786432 | tf_op jit(solution)/shard_map/all_to_all | solution.py:130
  224.4 8.7 %copy-start.10 = (f32[48,4,32]{0,2,1:T(8,128)S(1)}, f32[48,4,32]{0,2,1:T(8,128)}, u32[]{:S(2)}) copy-start(f32[48,4,32]{0,2,1:T(8,128)} %copy-done.9) | copy-start | bytes 73732
  224.4 9.6 %copy-start.1 = (bf16[48,384]{1,0:T(8,128)(2,1)S(1)}, bf16[48,384]{1,0:T(8,128)(2,1)}, u32[]{:S(2)}) copy-start(bf16[48,384]{1,0:T(8,128)(2,1)} %param.13) | copy-start | bytes 110596
Sparse Core Ops, SparseCore 0:
  27.9 82.6 all-gather.1
  129.8 84.8 reduce-scatter.1
where the time goes:
time: 241 us
  waiting for transfers between devices  157 us (65%)
  matrix products  33.3 us (14%)
  blocking collectives  15.8 us (7%)
  between operations  14.4 us (6%)
  starting transfers between devices  9.09 us (4%)
  other arithmetic  7.59 us (3%)
  local copies, waits for them, and re-layouts  3.4 us (1%)
    all_gather x1, waiting for transfers between devices, per_device(): mine_full = lax.all_gather(mine, TN, axis=2, tiled=True)  76.6 us
    reduce_scatter x1, waiting for transfers between devices, per_device(): scattered = lax.psum_scatter(summed, TN, scatter_dimension=0, tiled=True)  68.6 us
    all_to_all x1, blocking collectives, per_device(): recv = lax.all_to_all(send, SRC, split_axis=0, concat_axis=0, tiled=True)  15.8 us
    all_to_all x1, starting transfers between devices, per_device(): lax.all_to_all(done, SRC, split_axis=0, concat_axis=0, tiled=True)  7.54 us
    dot_general x2, matrix products, weight_grads(): jnp.einsum('rh,rd->hd', f[4], grads, preferred_element_type=jnp.float32)  6.88 us
    dot_general x2, matrix products, weight_grads(): jnp.einsum('rd,rh->dh', rows, b[1], preferred_element_type=jnp.float32)  5.32 us
    ppermute x2, waiting for transfers between devices, per_device(): gu_other, down_other = lax.ppermute((gu_local, down_local), 'core', pair)  5.15 us
    dot_general x2, matrix products, forward(): jnp.einsum('hd,rh->dr', down_w, hidden, preferred_element_type=jnp.float32)  5.07 us
  transfers between devices with their start and end apart: 8, of which 6 were waited for; matrix products, arithmetic and copies ran while one was open for 9% of the time, Pallas kernels for 0%

commit v1 on v0

--- a/solution.py
+++ b/solution.py
@@ -54,7 +54,9 @@
     recv = lax.all_to_all(send, SRC, split_axis=0, concat_axis=0, tiled=True)
     mine = recv.reshape(n_src, 2, CAP, feature_cols).transpose(1, 0, 2, 3)
     mine = mine.reshape(2, n_src * CAP, feature_cols)
-    mine_full = lax.all_gather(mine, TN, axis=2, tiled=True)
+    mine_full = jnp.concatenate(
+        lax.all_to_all(jnp.stack([mine] * lax.axis_size(TN)), TN, 0, 0), axis=2
+    )
     pair = [(0, 1), (1, 0)]
     gate_local = gate_matrix[0]
     up_local = up_matrix[0]

time: 241 us -> 325 us (1.35)
  waiting for transfers between devices: 157 us -> 217 us
  local copies, waits for them, and re-layouts: 3.4 us -> 15.9 us
  starting transfers between devices: 9.09 us -> 16.5 us
    all_to_all x0 -> x1, waiting for transfers between devices: none -> 136 us  [per_device(): lax.all_to_all(jnp.stack([mine] * lax.axis_size(TN)), TN, 0, 0)]
    all_gather x1 -> x0, waiting for transfers between devices: 76.6 us -> none  [per_device(): mine_full = lax.all_gather(mine, TN, axis=2, tiled=True)]
    all_to_all x0 -> x1, starting transfers between devices: none -> 8.9 us  [per_device(): lax.all_to_all(jnp.stack([mine] * lax.axis_size(TN)), TN, 0, 0)]
    reduce_scatter x1, waiting for transfers between devices: 68.6 us -> 74.3 us  [per_device(): scattered = lax.psum_scatter(summed, TN, scatter_dimension=0, tiled=True)]
    ppermute x2, waiting for transfers between devices: 5.15 us -> 0.01 us  [per_device(): gu_other, down_other = lax.ppermute((gu_local, down_local), 'core', pair)]
    another operation x0 -> x2, local copies, waits for them, and re-layouts: none -> 3.52 us  [per_device(): jnp.stack([mine] * lax.axis_size(TN))]
    dot_general x2, matrix products: 3.28 us -> 6.71 us  [weight_grads(): jnp.einsum('rd,rh->dh', rows, b[0], preferred_element_type=jnp.float32)]
  transfers between devices with their start and end apart: 8 -> 8, of which waited for: 6 -> 5; matrix products, arithmetic and copies ran while one was open for 9% -> 9% of each run, Pallas kernels for 0% -> 0%
where the time goes in v1:
time: 325 us; the launch traced here: 324 us
  waiting for transfers between devices  217 us (67%)
  matrix products  33.7 us (10%)
  starting transfers between devices  16.5 us (5%)
  local copies, waits for them, and re-layouts  15.9 us (5%)
  blocking collectives  15.8 us (5%)
  between operations  14.3 us (4%)
  other arithmetic  10.1 us (3%)
    all_to_all x1, waiting for transfers between devices, per_device(): lax.all_to_all(jnp.stack([mine] * lax.axis_size(TN)), TN, 0, 0)  136 us
    reduce_scatter x1, waiting for transfers between devices, per_device(): scattered = lax.psum_scatter(summed, TN, scatter_dimension=0, tiled=True)  74.3 us
    all_to_all x1, blocking collectives, per_device(): recv = lax.all_to_all(send, SRC, split_axis=0, concat_axis=0, tiled=True)  15.8 us
    all_to_all x1, starting transfers between devices, per_device(): lax.all_to_all(jnp.stack([mine] * lax.axis_size(TN)), TN, 0, 0)  8.9 us
    dot_general x2, matrix products, weight_grads(): jnp.einsum('rd,rh->dh', rows, b[0], preferred_element_type=jnp.float32)  6.71 us
  transfers between devices with their start and end apart: 8, of which 5 were waited for; matrix products, arithmetic and copies ran while one was open for 9% of the time, Pallas kernels for 0%

profile of v1, /device:TPU:8, one launch (start us, length us, event | category | flops | bytes accessed | tf_op | source)
XLA Modules:
  0.0 323.9 jit_solution(3678171571322285994)
XLA Ops:
  7.2 0.0 copy-start
  7.2 0.7 fusion.29
  7.9 0.1 copy.46
  8.0 0.1 reduce_window_sum.11
  8.1 0.1 copy.47
  8.1 0.7 convert_element_type.89
  8.8 0.7 select_reduce_fusion
  9.5 0.0 copy-start.9
  9.6 0.6 copy-done.9
  10.2 0.3 convolution_convert_fusion.5
  10.5 1.0 convolution_convert_fusion.4
  11.5 15.8 %all_to_all.15 = bf16[8,64,384]{2,1,0:T(8,128)(2,1)S(1)} all-to-all(bf16[8,64,384]{2,1,0:T(8,128)(2,1)S(1)} %pad_maximum_fusion.1), channel_id=1, replica_groups=mesh['y'=4,'xhi'=2,'core'=2,'xlo'=2,'z'=8] {'y','xhi'}, dimensions={0} | all-to-all | bytes 786432 | tf_op jit(solution)/shard_map/all_to_all | solution.py:54
  27.4 0.2 copy.49
  27.6 3.3 %stack.3 = bf16[16,2,256,384]{2,3,1,0:T(8,128)(2,1)} broadcast(bf16[2,256,384]{1,2,0:T(8,128)(2,1)S(1)} %copy.49), dimensions={1,2,3} | broadcast | bytes 6684672 | tf_op jit(solution)/shard_map/stack | solution.py:58
  30.9 8.9 %all-to-all-start.1 = ((bf16[16,2,256,384]{2,3,1,0:T(8,128)(2,1)}), bf16[16,2,256,384]{2,3,1,0:T(8,128)(2,1)}, u32[]{:S(2)}, u32[]{:S(2)}) async-start(bf16[16,2,256,384]{2,3,1,0:T(8,128)(2,1)} %stack.3), calls=%async_computation.1 | async-start | bytes 12582912 | tf_op jit(solution)/shard_map/all_to_all | solution.py:58
  39.8 0.0 reduce-scatter.2.cloned.1.call-start
  39.9 0.0 copy-done.4
  39.9 0.0 copy-done.6
  39.9 2.0 pad_maximum_fusion
  41.9 0.0 collective-permute-start
  41.9 0.5 collective-permute-start.1
  42.4 135.8 %all-to-all-done.1 = bf16[16,2,256,384]{2,3,1,0:T(8,128)(2,1)} async-done(((bf16[16,2,256,384]{2,3,1,0:T(8,128)(2,1)}), bf16[16,2,256,384]{2,3,1,0:T(8,128)(2,1)}, u32[]{:S(2)}, u32[]{:S(2)}) %all-to-all-start.1) | async-done | bytes 6291488 | tf_op jit(solution)/shard_map/all_to_all | solution.py:58
  178.2 3.2 copy.57
  181.4 0.0 copy-start.5
  181.4 0.0 copy-start.7
  181.4 0.4 fusion.35
  181.9 0.0 collective-permute-done
  181.9 1.0 copy-done.5
  182.9 1.6 copy-done.7
  184.4 3.6 %fusion.8 = f32[256,512]{1,0:T(8,128)S(1)} fusion(bf16[256,6144]{0,1:T(8,128)(2,1)S(1)} %bitcast.63, bf16[6144,256]{1,0:T(8,128)(2,1)} %collective-permute-done, bf16[6144,128]{1,0:T(8,128)(2,1)S(1)} %bitcast.75, bf16[6144,128]{1,0:T(8,128)(2,1)S(1)} %bitcast.78), kind=kOutput, calls=%fused_computation.16 | convolution fusion | flops 1629487104 | bytes 9961472 | tf_op jit(solution)/shard_map/dot_general | solution.py:95
  188.1 0.0 collective-permute-done.1
  188.1 3.0 fusion.14
  191.0 0.2 multiply_convert_fusion.1
  191.2 0.0 copy-start.12
  191.3 0.0 copy-start.8
  191.3 2.5 fusion
  193.8 1.0 convolution_convert_fusion.2
  194.8 2.4 fusion.1
  197.3 2.9 convolution_convert_fusion
  200.2 3.9 %add_convert_fusion = bf16[6144,512]{1,0:T(8,128)(2,1)} fusion(bf16[6144,256]{1,0:T(8,128)(2,1)S(1)} %convolution_convert_fusion.2, bf16[6144,256]{1,0:T(8,128)(2,1)S(1)} %fusion, bf16[6144,256]{1,0:T(8,128)(2,1)S(1)} %convolution_convert_fusion, bf16[6144,256]{1,0:T(8,128)(2,1)S(1)} %fusion.1), kind=kLoop, calls=%fused_computation | loop fusion | flops 31457280 | bytes 18874368 | tf_op jit(solution)/shard_map/convert_element_type | solution.py:110
  204.1 0.0 reduce-scatter.2.cloned.1.call-update
  204.1 3.1 fusion.39
  207.2 0.1 collective-permute-start.4
  207.3 1.0 fusion.38
  208.3 0.6 collective-permute-start.3
  208.8 2.6 fusion.37
  211.5 0.0 collective-permute-start.2
  211.5 1.4 collective-permute-done.4
  212.9 2.3 fusion.5
  215.2 2.2 collective-permute-done.3
  217.4 2.1 fusion.6
  219.5 74.3 %reduce-scatter.2.cloned.1.call-done = bf16[384,512]{1,0:T(8,128)(2,1)} async-done(((bf16[6144,512]{1,0:T(8,128)(2,1)}), bf16[384,512]{1,0:T(8,128)(2,1)}) %reduce-scatter.2.cloned.1.call-update) | async-done | bytes 393232 | tf_op jit(solution)/shard_map/reduce_scatter | solution.py:111
  293.8 1.7 slice_bitcast_fusion.1
  295.6 1.7 copy.53
  297.3 0.8 copy.54
  298.1 1.8 pad_maximum_fusion.2
  299.9 6.4 %all-to-all-start.2 = ((bf16[8,64,384]{2,1,0:T(8,128)(2,1)}), bf16[8,64,384]{2,1,0:T(8,128)(2,1)}, u32[]{:S(2)}, u32[]{:S(2)}) async-start(bf16[8,64,384]{2,1,0:T(8,128)(2,1)} %pad_maximum_fusion.2), calls=%async_computation.3 | async-start | bytes 786432 | tf_op jit(solution)/shard_map/all_to_all | solution.py:132
  306.3 0.0 collective-permute-done.2
  306.3 0.0 copy-start.1
  306.3 4.1 %fusion.7 = bf16[1,6144,128]{2,1,0:T(8,128)(2,1)} fusion(f32[6144,128]{1,0:T(8,128)} %collective-permute-done.2, bf16[256,6144]{0,1:T(8,128)(2,1)S(1)} %bitcast.67, bf16[256,128]{1,0:T(8,128)(2,1)} %copy-done.11), kind=kOutput, calls=%fused_computation.15 | convolution fusion | flops 404226048 | bytes 7929856 | tf_op jit(solution)/shard_map/rd,rh->dh/dot_general | solution.py:118
  310.4 3.7 %all-to-all-done.2 = bf16[8,64,384]{2,1,0:T(8,128)(2,1)} async-done(((bf16[8,64,384]{2,1,0:T(8,128)(2,1)}), bf16[8,64,384]{2,1,0:T(8,128)(2,1)}, u32[]{:S(2)}, u32[]{:S(2)}) %all-to-all-start.2) | async-done | bytes 393248 | tf_op jit(solution)/shard_map/all_to_all | solution.py:132
  314.1 1.1 fusion.36
  315.2 0.9 convolution_convert_fusion.7
  316.1 0.9 convolution_convert_fusion.6
  (25 shorter events, 0.2 us)
Async XLA Ops:
  7.2 3.0 copy-start
  9.5 0.6 copy-start.9
  30.9 9.0 %copy-start.4 = (bf16[1,6144,128]{2,1,0:T(8,128)(2,1)S(1)}, bf16[1,6144,128]{2,1,0:T(8,128)(2,1)}, u32[]{:S(2)}) copy-start(bf16[1,6144,128]{2,1,0:T(8,128)(2,1)} %param.11) | copy-start | bytes 4718596
  30.9 9.0 %copy-start.6 = (bf16[1,6144,128]{2,1,0:T(8,128)(2,1)S(1)}, bf16[1,6144,128]{2,1,0:T(8,128)(2,1)}, u32[]{:S(2)}) copy-start(bf16[1,6144,128]{2,1,0:T(8,128)(2,1)} %param.10) | copy-start | bytes 4718596
  30.9 147.3 %all-to-all-start.1 = ((bf16[16,2,256,384]{2,3,1,0:T(8,128)(2,1)}), bf16[16,2,256,384]{2,3,1,0:T(8,128)(2,1)}, u32[]{:S(2)}, u32[]{:S(2)}) async-start(bf16[16,2,256,384]{2,3,1,0:T(8,128)(2,1)} %stack.3), calls=%async_computation.1 | async-start | bytes 12582912 | tf_op jit(solution)/shard_map/all_to_all | solution.py:58
  39.8 254.0 %reduce-scatter.2.cloned.1.call-start = ((), (), s32[]{:S(2)}) async-start(), calls=%async_computation.4 | async-start | bytes 6684672 | tf_op jit(solution)/shard_map/reduce_scatter | solution.py:111
  41.9 140.0 %collective-permute-start = (bf16[6144,256]{1,0:T(8,128)(2,1)}, bf16[6144,256]{1,0:T(8,128)(2,1)}, u32[]{:S(2)}, u32[]{:S(2)}) collective-permute-start(bf16[6144,256]{1,0:T(8,128)(2,1)} %pad_maximum_fusion), channel_id=1, source_target_pairs={{0,16},{16,0},{1,17},{17,1},{2,18},{18,2},{3,19},{19,3},{4,20},{20... | collective-permute-start | bytes 9437192 | tf_op jit(solution)/shard_map/ppermute | solution.py:65
  41.9 146.2 %collective-permute-start.1 = (bf16[128,6144]{1,0:T(8,128)(2,1)}, bf16[128,6144]{1,0:T(8,128)(2,1)}, u32[]{:S(2)}, u32[]{:S(2)}) collective-permute-start(bf16[128,6144]{1,0:T(8,128)(2,1)} %bitcast.11), channel_id=1, source_target_pairs={{0,16},{16,0},{1,17},{17,1},{2,18},{18,2},{3,19},{19,3},{4,20},{20... | collective-permute-start | bytes 4718600 | tf_op jit(solution)/shard_map/ppermute | solution.py:65
  181.4 1.5 copy-start.5
  181.4 3.0 copy-start.7
  181.9 6.2 %copy-start.2 = (bf16[1,256,16,384]{1,3,2,0:T(8,128)(2,1)}, bf16[1,256,16,384]{1,3,2,0:T(8,128)(2,1)S(1)}, u32[]{:S(2)}) copy-start(bf16[1,256,16,384]{1,3,2,0:T(8,128)(2,1)S(1)} %get-tuple-element.6) | copy-start | bytes 9437188
  191.2 3.6 %copy-start.11 = (bf16[256,128]{1,0:T(8,128)(2,1)}, bf16[256,128]{1,0:T(8,128)(2,1)S(1)}, u32[]{:S(2)}) copy-start(bf16[256,128]{1,0:T(8,128)(2,1)S(1)} %get-tuple-element.10) | copy-start | bytes 196612
  191.2 3.6 %copy-start.12 = (bf16[256,128]{1,0:T(8,128)(2,1)}, bf16[256,128]{1,0:T(8,128)(2,1)S(1)}, u32[]{:S(2)}) copy-start(bf16[256,128]{1,0:T(8,128)(2,1)S(1)} %get-tuple-element.8) | copy-start | bytes 196612
  191.3 3.6 %copy-start.8 = (bf16[256,128]{1,0:T(8,128)(2,1)}, bf16[256,128]{1,0:T(8,128)(2,1)S(1)}, u32[]{:S(2)}) copy-start(bf16[256,128]{1,0:T(8,128)(2,1)S(1)} %get-tuple-element.11) | copy-start | bytes 196612
  207.2 5.7 %collective-permute-start.4 = (f32[128,6144]{1,0:T(8,128)S(1)}, f32[128,6144]{1,0:T(8,128)S(1)}, u32[]{:S(2)}, u32[]{:S(2)}) collective-permute-start(f32[128,6144]{1,0:T(8,128)S(1)} %fusion.39), channel_id=1, source_target_pairs={{0,16},{16,0},{1,17},{17,1},{2,18},{18,2},{3,19},{19,3},{4,20},{20... | collective-permute-start | bytes 9437192 | tf_op jit(solution)/shard_map/ppermute | solution.py:124
  208.3 4.7 %copy-start.3 = (bf16[1,256,16,384]{1,3,2,0:T(8,128)(2,1)S(1)}, bf16[1,256,16,384]{1,3,2,0:T(8,128)(2,1)}, u32[]{:S(2)}) copy-start(bf16[1,256,16,384]{1,3,2,0:T(8,128)(2,1)} %copy-done.2) | copy-start | bytes 9437188
  208.3 9.2 %collective-permute-start.3 = (f32[6144,128]{1,0:T(8,128)S(1)}, f32[6144,128]{1,0:T(8,128)S(1)}, u32[]{:S(2)}, u32[]{:S(2)}) collective-permute-start(f32[6144,128]{1,0:T(8,128)S(1)} %fusion.38), channel_id=1, source_target_pairs={{0,16},{16,0},{1,17},{17,1},{2,18},{18,2},{3,19},{19,3},{4,20},{20... | collective-permute-start | bytes 9437192 | tf_op jit(solution)/shard_map/ppermute | solution.py:124
  211.5 5.9 %copy-start.13 = (bf16[256,128]{1,0:T(8,128)(2,1)S(1)}, bf16[256,128]{1,0:T(8,128)(2,1)}, u32[]{:S(2)}) copy-start(bf16[256,128]{1,0:T(8,128)(2,1)} %copy-done.12) | copy-start | bytes 196612
  211.5 94.8 %collective-permute-start.2 = (f32[6144,128]{1,0:T(8,128)}, f32[6144,128]{1,0:T(8,128)}, u32[]{:S(2)}, u32[]{:S(2)}) collective-permute-start(f32[6144,128]{1,0:T(8,128)} %fusion.37), channel_id=1, source_target_pairs={{0,16},{16,0},{1,17},{17,1},{2,18},{18,2},{3,19},{19,3},{4,20},{20... | collective-permute-start | bytes 9437192 | tf_op jit(solution)/shard_map/ppermute | solution.py:124
  299.9 14.2 %all-to-all-start.2 = ((bf16[8,64,384]{2,1,0:T(8,128)(2,1)}), bf16[8,64,384]{2,1,0:T(8,128)(2,1)}, u32[]{:S(2)}, u32[]{:S(2)}) async-start(bf16[8,64,384]{2,1,0:T(8,128)(2,1)} %pad_maximum_fusion.2), calls=%async_computation.3 | async-start | bytes 786432 | tf_op jit(solution)/shard_map/all_to_all | solution.py:132
  306.3 9.8 %copy-start.10 = (f32[48,4,32]{0,2,1:T(8,128)S(1)}, f32[48,4,32]{0,2,1:T(8,128)}, u32[]{:S(2)}) copy-start(f32[48,4,32]{0,2,1:T(8,128)} %copy-done.9) | copy-start | bytes 73732
  306.3 10.7 %copy-start.1 = (bf16[48,384]{1,0:T(8,128)(2,1)S(1)}, bf16[48,384]{1,0:T(8,128)(2,1)}, u32[]{:S(2)}) copy-start(bf16[48,384]{1,0:T(8,128)(2,1)} %param.13) | copy-start | bytes 110596
Sparse Core Ops, SparseCore 0:
  204.2 89.5 reduce-scatter.1
